TPU v7x, 32 devices: a whole 2x2x4 slice. The times are simulated.
32 devices in a mesh: req: 16 (over z, x, core), ep: 2 (over y).
Axes of the slice: x: 2, y: 2, z: 4, core: 2. Of those that a mesh axis runs over, the one named last changes fastest.
Arguments:
- hidden: bfloat16 [16, 512, 1536], P('req', None, 'ep'), may hold values from -6 to 6
- key_cache: bfloat16 [16, 8, 2560, 64], P('req', 'ep'), may hold values from -160 to 160
- value_cache: bfloat16 [16, 8, 2560, 64], P('req', 'ep'), may hold values from -6 to 6
- request_order: int32 [16], replicated, may hold values from 0 to 15, each once
- cached_lengths: int32 [16], replicated, may hold values from 1 to 2048, 16384 in all
- expert_ids: int32 [16, 512, 8], P('req'), may hold values from 0 to 39, all different within a row; in each aligned block of 512 rows (0 to 511, 512 to 1023, ..., all dimensions but the last counted through in order) at most 192 rows name the same one
- gate_values: float32 [16, 512, 8], P('req'), may hold values from 0.1 to 1
- attn_gain: float32 [1536], replicated, may hold values from 0.25 to 1.75
- ffn_gain: float32 [1536], replicated, may hold values from 0.25 to 1.75
- w_query: bfloat16 [1536, 1536], P(None, 'ep'), may hold values from -0.15625 to 0.15625
- w_key: bfloat16 [1536, 512], P(None, 'ep'), may hold values from -0.15625 to 0.15625
- w_value: bfloat16 [1536, 512], P(None, 'ep'), may hold values from -0.15625 to 0.15625
- w_out: bfloat16 [1536, 1536], P('ep'), may hold values from -0.15625 to 0.15625
- expert_gate: bfloat16 [4, 1536, 512], P('ep', 'req'), may hold values from -0.15625 to 0.15625
- expert_up: bfloat16 [4, 1536, 512], P('ep', 'req'), may hold values from -0.15625 to 0.15625
- expert_down: bfloat16 [4, 512, 1536], P('ep', 'req'), may hold values from -0.25 to 0.25
Outputs:
- hidden_out: bfloat16 [16, 512, 1536], P('req', None, 'ep')
- key_cache_out: bfloat16 [16, 8, 2560, 64], P('req', 'ep')
- value_cache_out: bfloat16 [16, 8, 2560, 64], P('req', 'ep')
Inputs may be any that keep to these rules, and one draw needn't show every extreme that they name: Slot s holds request request_order[s]; every request is held by one slot. `cached_lengths`: the longest cached length is exactly 2048. `expert_ids`: each token names 8 different experts; among the 512 tokens of one slot no expert is named by more than 192 tokens, a bound that some block reaches.
All inputs are finite; a program needn't handle non-finite values.
Results may differ from a plain program's by a relative error of at most 0.012.
The roundings to bfloat16 on the way count: a program that leaves them out, or rounds other values in their place, can miss the bound.
Values may be sent and summed in bfloat16 or wider, within the bound.
No kernel may reach another device: no remote copies, remote signals or barrier semaphores. Data moves between devices by JAX's collectives and lax.ppermute only.
A program may use at most 128 MiB of HBM per device.

v0:
```python
import jax
import jax.numpy as jnp
from jax import lax
from jax.sharding import PartitionSpec as P

epsilon = 1e-06


def normalize(values, gain):
    return values * lax.rsqrt(jnp.mean(values * values, -1, keepdims=True) + epsilon) * gain


def rotate(values, positions):
    half = values.shape[-1] // 2
    freq = 10000.0 ** (-jnp.arange(half, dtype=jnp.float32) * (2.0 / values.shape[-1]))
    angle = positions.astype(jnp.float32)[:, None] * freq[None, :]
    cosine = jnp.cos(angle)
    sine = jnp.sin(angle)
    first = values[..., :half]
    second = values[..., half:]
    return jnp.concatenate([first * cosine - second * sine, second * cosine + first * sine], -1)


def rounded(values):
    return lax.optimization_barrier(values.astype(jnp.bfloat16)).astype(jnp.float32)


def route_tables(chosen, gate_rows, wanted, capacity):
    hits = chosen[:, :, None] == wanted[None, None, :]
    member = jnp.sum(hits.astype(jnp.int32), 1, dtype=jnp.int32)
    weight = jnp.sum(jnp.where(hits, gate_rows[:, :, None], 0.0), 1)
    place = jnp.cumsum(member, 0, dtype=jnp.int32) - 1
    slots = jnp.arange(capacity, dtype=jnp.int32)
    table = (member.T[:, None, :] == 1) & (place.T[:, None, :] == slots[None, :, None])
    gate_slot = jnp.sum(jnp.where(table, weight.T[:, None, :], 0.0), 2)
    return (table.astype(jnp.bfloat16), gate_slot)


def attend(query, keys, values, length, new_rows):
    query_rows = query.shape[1]
    blocks = keys.shape[1] // new_rows
    limit = length + jnp.arange(query_rows, dtype=jnp.int32) % new_rows
    scale = query.shape[2] ** (-0.5)

    def visit(carry, block):
        running, total, summed = carry
        start = block * new_rows
        key_block = lax.dynamic_slice_in_dim(keys, start, new_rows, 1)
        value_block = lax.dynamic_slice_in_dim(values, start, new_rows, 1)
        scores = (
            jnp.einsum("kqd,kjd->kqj", query, key_block, preferred_element_type=jnp.float32) * scale
        )
        column = start + jnp.arange(new_rows, dtype=jnp.int32)
        visible = column[None, :] <= limit[:, None]
        scores = jnp.where(visible[None], scores, -1e30)
        highest = jnp.maximum(running, jnp.max(scores, -1))
        correction = jnp.exp(running - highest)
        probs = jnp.where(visible[None], jnp.exp(scores - highest[..., None]), 0.0)
        total = total * correction + jnp.sum(probs, -1)
        summed = summed * correction[..., None] + jnp.einsum(
            "kqj,kjd->kqd",
            probs.astype(jnp.bfloat16),
            value_block,
            preferred_element_type=jnp.float32,
        )
        return ((highest, total, summed), None)

    start_state = (
        jnp.full(query.shape[:2], -1e30, jnp.float32),
        jnp.zeros(query.shape[:2], jnp.float32),
        jnp.zeros(query.shape, jnp.float32),
    )
    final, unused = lax.scan(visit, start_state, jnp.arange(blocks, dtype=jnp.int32))
    return final[2] / final[1][..., None]


def on_device(
    hidden,
    key_cache,
    value_cache,
    request_order,
    cached_lengths,
    expert_ids,
    gate_values,
    attn_gain,
    ffn_gain,
    w_query,
    w_key,
    w_value,
    w_out,
    expert_gate,
    expert_up,
    expert_down,
):
    own_rows = hidden[0]
    new_rows = own_rows.shape[0]
    own_width = own_rows.shape[1]
    head_dim = key_cache.shape[3]
    kv_local = key_cache.shape[1]
    heads_local = w_query.shape[1] // head_dim
    group = heads_local // kv_local
    per_device = expert_gate.shape[0]
    devices = lax.axis_size("ep")
    capacity = 3 * new_rows // 8
    everyone = jnp.arange(request_order.shape[0], dtype=jnp.int32)
    request = jnp.sum(jnp.where(everyone == lax.axis_index("req"), request_order, 0))
    length = jnp.sum(jnp.where(everyone == request, cached_lengths, 0))
    rows_whole = lax.all_gather(own_rows, "ep", axis=1, tiled=True)
    width = rows_whole.shape[1]
    normed = normalize(rows_whole.astype(jnp.float32), attn_gain).astype(jnp.bfloat16)
    query = jnp.dot(normed, w_query, preferred_element_type=jnp.float32)
    key_new = jnp.dot(normed, w_key, preferred_element_type=jnp.float32)
    value_new = jnp.dot(normed, w_value, preferred_element_type=jnp.float32)
    positions = length + jnp.arange(new_rows, dtype=jnp.int32)
    query = rotate(
        query.reshape(new_rows, heads_local, head_dim).transpose(1, 0, 2), positions
    ).astype(jnp.bfloat16)
    query = query.reshape(kv_local, group * new_rows, head_dim)
    key_new = rotate(
        key_new.reshape(new_rows, kv_local, head_dim).transpose(1, 0, 2), positions
    ).astype(jnp.bfloat16)
    value_new = (
        value_new.reshape(new_rows, kv_local, head_dim).transpose(1, 0, 2).astype(jnp.bfloat16)
    )
    zero = jnp.zeros((), jnp.int32)
    keys = lax.dynamic_update_slice(key_cache[0], key_new, (zero, length, zero))
    values = lax.dynamic_update_slice(value_cache[0], value_new, (zero, length, zero))
    attended = attend(query, keys, values, length, new_rows)
    attended = (
        attended.reshape(heads_local, new_rows, head_dim)
        .transpose(1, 0, 2)
        .reshape(new_rows, heads_local * head_dim)
        .astype(jnp.bfloat16)
    )
    partial_value = rounded(jnp.dot(attended, w_out, preferred_element_type=jnp.float32))
    head_sum = lax.psum_scatter(
        partial_value.astype(jnp.bfloat16), "ep", scatter_dimension=1, tiled=True
    ).astype(jnp.float32)
    mixed = (own_rows.astype(jnp.float32) + head_sum).astype(jnp.bfloat16)
    mixed_f = mixed.astype(jnp.float32)
    chosen = expert_ids[0]
    gate_rows = gate_values[0]
    first = lax.axis_index("ep") * per_device
    squares = jnp.sum(mixed_f * mixed_f, -1)
    totals = lax.psum(squares, "ep")
    local_gain = lax.dynamic_slice_in_dim(ffn_gain, lax.axis_index("ep") * own_width, own_width)
    normed_cols = (mixed_f * lax.rsqrt(totals / width + epsilon)[:, None] * local_gain).astype(
        jnp.bfloat16
    )
    table_all, gate_all = route_tables(
        chosen, gate_rows, jnp.arange(per_device * devices, dtype=jnp.int32), capacity
    )
    buffers = jnp.einsum(
        "ect,td->ecd", table_all, normed_cols, preferred_element_type=jnp.float32
    ).astype(jnp.bfloat16)
    inputs = lax.all_to_all(buffers, "ep", split_axis=0, concat_axis=2, tiled=True)
    gate_own = lax.dynamic_slice_in_dim(gate_all, first, per_device, 0)
    columns = inputs
    gate_next = jnp.einsum(
        "ecd,edf->ecf",
        columns,
        lax.all_gather(expert_gate, "req", axis=1, tiled=True),
        preferred_element_type=jnp.float32,
    )
    up_next = jnp.einsum(
        "ecd,edf->ecf",
        columns,
        lax.all_gather(expert_up, "req", axis=1, tiled=True),
        preferred_element_type=jnp.float32,
    )
    hidden_act = (jax.nn.silu(gate_next) * up_next).astype(jnp.bfloat16)
    columns = hidden_act
    output = jnp.einsum(
        "ecf,efd->ecd",
        columns,
        lax.all_gather(expert_down, "req", axis=1, tiled=True),
        preferred_element_type=jnp.float32,
    )
    contrib = (output * gate_own[..., None]).astype(jnp.bfloat16)
    returned = lax.all_to_all(contrib, "ep", split_axis=2, concat_axis=0, tiled=True)
    per_expert = jnp.einsum("ect,ecd->etd", table_all, returned, preferred_element_type=jnp.float32)
    grouped = rounded(jnp.sum(per_expert.reshape(devices, per_device, new_rows, own_width), 1))
    expert_sum = jnp.sum(grouped, 0)
    result = (mixed_f + expert_sum).astype(jnp.bfloat16)
    return (result[None], keys[None], values[None])


def solution(mesh):
    in_specs = (
        P("req", None, "ep"),
        P("req", "ep", None, None),
        P("req", "ep", None, None),
        P(),
        P(),
        P("req", None, None),
        P("req", None, None),
        P(),
        P(),
        P(None, "ep"),
        P(None, "ep"),
        P(None, "ep"),
        P("ep", None),
        P("ep", "req", None),
        P("ep", "req", None),
        P("ep", "req", None),
    )
    out_specs = (P("req", None, "ep"), P("req", "ep", None, None), P("req", "ep", None, None))
    return jax.shard_map(
        on_device, mesh=mesh, in_specs=in_specs, out_specs=out_specs, check_vma=False
    )
```

profile of v0, /device:TPU:0, one launch (start us, length us, event | category | flops | bytes accessed | tf_op | source)
XLA Modules:
  0.0 390.4 jit_solution(1194642636352865639)
XLA Ops:
  8.1 2.6 copy.81
  10.7 1.1 copy.82
  12.5 1.3 fusion.60
  16.7 25.2 %all-gather.12.cloned.1.call-done = bf16[1,512,1536]{2,1,0:T(8,128)(2,1)} async-done(((bf16[1,512,768]{2,1,0:T(8,128)(2,1)}), bf16[1,512,1536]{2,1,0:T(8,128)(2,1)}) %all-gather.12.cloned.1.call-update) | async-done | bytes 1572880 | tf_op jit(solution)/shard_map/all_gather | solution.py:108
  41.8 1.9 fusion.24
  43.8 2.1 fusion.66
  46.0 1.6 fusion.64
  47.5 1.0 subtract_convert_fusion
  48.8 1.1 concatenate.14
  49.8 1.2 copy.52
  51.0 1.1 concatenate.15
  52.1 1.6 pad_maximum_fusion
  53.8 1.0 copy.53
  54.8 4.0 %dynamic_update_slice.6 = bf16[4,2560,64]{1,2,0:T(8,128)(2,1)} dynamic-update-slice(bf16[4,2560,64]{1,2,0:T(8,128)(2,1)} %bitcast.102, bf16[4,512,64]{1,2,0:T(8,128)(2,1)S(1)} %pad_maximum_fusion.1, s32[]{:T(128)} %constant.31.clone.1, s32[]{:T(128)S(6)} %select_n.46, s32[]{:T(128)} %constant.31.clone.1) | dynamic-update-slice | bytes 524292 | tf_op jit(solution)/shard_map/dynamic_update_slice | solution.py:126
  58.8 2.4 convolution_convert_fusion.1
  61.1 3.8 dynamic_update_slice.7
  64.9 123.9 %while.15 = (s32[]{:T(128)}, f32[4,1536]{1,0:T(4,128)S(1)}, f32[4,1536]{1,0:T(4,128)S(1)}, f32[4,1536,64]{1,2,0:T(8,128)}, s32[5]{0:T(128)S(1)}, /*index=5*/bf16...) while((s32[]{:T(128)}, f32[4,1536]{1,0:T(4,128)S(1)}, ...), condition=%wide.region_6.7_spmd.clone, body=%wide.region_3.6_spmd.clone.sunk | while | flops 848208896 | bytes 96092400 | solution.py:73
  64.9 0.7 dynamic_slice.33
  67.5 8.1 %fusion.93 = (f32[4,1536]{1,0:T(4,128)S(1)}, f32[4,512,1536]{2,1,0:T(8,128)}) fusion(pred[1536,512]{0,1:T(8,128)(4,1)S(1)} %broadcast_compare_fusion.3, bf16[4,1536,64]{1,2,0:T(8,128)(2,1)} %get-tuple-element.236, bf16[4,2560,64]{1,2,0:T(8,128)(2,1)} %get-tuple-element.235, s32[]{:T(128)S(6)} %select_n.102), kind=kOutput, calls=%fused_computation.3.clone.1 | convolution fusion | flops 412084224 | bytes 14442500 | tf_op jit(solution)/shard_map/while/body/eval_jaxpr/kqd,kjd->kqj/dot_general | solution.py:51
  75.6 6.9 %fusion.94 = f32[4,1536]{1,0:T(4,128)S(1)} fusion(f32[4,512,1536]{2,1,0:T(8,128)} %get-tuple-element.201, f32[4,1536]{1,0:T(4,128)S(1)} %select_maximum_fusion.2, pred[1536,512]{0,1:T(8,128)(4,1)S(1)} %broadcast_compare_fusion.3), kind=kLoop, calls=%fused_computation.5.clone.1 | loop fusion | flops 15722496 | bytes 13418496 | tf_op jit(solution)/shard_map/while/body/eval_jaxpr/reduce_sum | solution.py:59
  82.5 1.4 copy-done.1
  83.8 5.7 %fusion.96 = f32[4,1536,64]{1,2,0:T(8,128)} fusion(f32[4,512,1536]{2,1,0:T(8,128)S(1)} %copy-done.1, f32[4,1536]{1,0:T(4,128)S(1)} %select_maximum_fusion.2, pred[1536,512]{0,1:T(8,128)(4,1)S(1)} %broadcast_compare_fusion.3, f32[4,1536,64]{1,2,0:T(8,128)} %get-tuple-element.220, f32[4,1536]{1,0:T(4,128)S(1)} %get-tuple-element.203, pred[]{:T(512)S(6)} %compare.4, ...), kind=kOutput, calls=%fused_computation.8.clone.1 | convolution fusion | flops 419561472 | bytes 16826372 | tf_op jit(solution)/shard_map/while/body/eval_jaxpr/kqj,kjd->kqd/dot_general | solution.py:60
  89.5 0.7 dynamic_slice.33
  92.1 8.1 %fusion.93 = (f32[4,1536]{1,0:T(4,128)S(1)}, f32[4,512,1536]{2,1,0:T(8,128)}) fusion(pred[1536,512]{0,1:T(8,128)(4,1)S(1)} %broadcast_compare_fusion.3, bf16[4,1536,64]{1,2,0:T(8,128)(2,1)} %get-tuple-element.236, bf16[4,2560,64]{1,2,0:T(8,128)(2,1)} %get-tuple-element.235, s32[]{:T(128)S(6)} %select_n.102), kind=kOutput, calls=%fused_computation.3.clone.1 | convolution fusion | flops 412084224 | bytes 14442500 | tf_op jit(solution)/shard_map/while/body/eval_jaxpr/kqd,kjd->kqj/dot_general | solution.py:51
  100.1 6.9 %fusion.94 = f32[4,1536]{1,0:T(4,128)S(1)} fusion(f32[4,512,1536]{2,1,0:T(8,128)} %get-tuple-element.201, f32[4,1536]{1,0:T(4,128)S(1)} %select_maximum_fusion.2, pred[1536,512]{0,1:T(8,128)(4,1)S(1)} %broadcast_compare_fusion.3), kind=kLoop, calls=%fused_computation.5.clone.1 | loop fusion | flops 15722496 | bytes 13418496 | tf_op jit(solution)/shard_map/while/body/eval_jaxpr/reduce_sum | solution.py:59
  107.0 1.4 copy-done.1
  108.4 6.0 %fusion.96 = f32[4,1536,64]{1,2,0:T(8,128)} fusion(f32[4,512,1536]{2,1,0:T(8,128)S(1)} %copy-done.1, f32[4,1536]{1,0:T(4,128)S(1)} %select_maximum_fusion.2, pred[1536,512]{0,1:T(8,128)(4,1)S(1)} %broadcast_compare_fusion.3, f32[4,1536,64]{1,2,0:T(8,128)} %get-tuple-element.220, f32[4,1536]{1,0:T(4,128)S(1)} %get-tuple-element.203, pred[]{:T(512)S(6)} %compare.4, ...), kind=kOutput, calls=%fused_computation.8.clone.1 | convolution fusion | flops 419561472 | bytes 16826372 | tf_op jit(solution)/shard_map/while/body/eval_jaxpr/kqj,kjd->kqd/dot_general | solution.py:60
  114.4 0.7 dynamic_slice.33
  116.9 8.1 %fusion.93 = (f32[4,1536]{1,0:T(4,128)S(1)}, f32[4,512,1536]{2,1,0:T(8,128)}) fusion(pred[1536,512]{0,1:T(8,128)(4,1)S(1)} %broadcast_compare_fusion.3, bf16[4,1536,64]{1,2,0:T(8,128)(2,1)} %get-tuple-element.236, bf16[4,2560,64]{1,2,0:T(8,128)(2,1)} %get-tuple-element.235, s32[]{:T(128)S(6)} %select_n.102), kind=kOutput, calls=%fused_computation.3.clone.1 | convolution fusion | flops 412084224 | bytes 14442500 | tf_op jit(solution)/shard_map/while/body/eval_jaxpr/kqd,kjd->kqj/dot_general | solution.py:51
  125.0 6.9 %fusion.94 = f32[4,1536]{1,0:T(4,128)S(1)} fusion(f32[4,512,1536]{2,1,0:T(8,128)} %get-tuple-element.201, f32[4,1536]{1,0:T(4,128)S(1)} %select_maximum_fusion.2, pred[1536,512]{0,1:T(8,128)(4,1)S(1)} %broadcast_compare_fusion.3), kind=kLoop, calls=%fused_computation.5.clone.1 | loop fusion | flops 15722496 | bytes 13418496 | tf_op jit(solution)/shard_map/while/body/eval_jaxpr/reduce_sum | solution.py:59
  131.9 1.4 copy-done.1
  133.2 6.0 %fusion.96 = f32[4,1536,64]{1,2,0:T(8,128)} fusion(f32[4,512,1536]{2,1,0:T(8,128)S(1)} %copy-done.1, f32[4,1536]{1,0:T(4,128)S(1)} %select_maximum_fusion.2, pred[1536,512]{0,1:T(8,128)(4,1)S(1)} %broadcast_compare_fusion.3, f32[4,1536,64]{1,2,0:T(8,128)} %get-tuple-element.220, f32[4,1536]{1,0:T(4,128)S(1)} %get-tuple-element.203, pred[]{:T(512)S(6)} %compare.4, ...), kind=kOutput, calls=%fused_computation.8.clone.1 | convolution fusion | flops 419561472 | bytes 16826372 | tf_op jit(solution)/shard_map/while/body/eval_jaxpr/kqj,kjd->kqd/dot_general | solution.py:60
  139.2 0.7 dynamic_slice.33
  141.7 8.1 %fusion.93 = (f32[4,1536]{1,0:T(4,128)S(1)}, f32[4,512,1536]{2,1,0:T(8,128)}) fusion(pred[1536,512]{0,1:T(8,128)(4,1)S(1)} %broadcast_compare_fusion.3, bf16[4,1536,64]{1,2,0:T(8,128)(2,1)} %get-tuple-element.236, bf16[4,2560,64]{1,2,0:T(8,128)(2,1)} %get-tuple-element.235, s32[]{:T(128)S(6)} %select_n.102), kind=kOutput, calls=%fused_computation.3.clone.1 | convolution fusion | flops 412084224 | bytes 14442500 | tf_op jit(solution)/shard_map/while/body/eval_jaxpr/kqd,kjd->kqj/dot_general | solution.py:51
  149.8 6.9 %fusion.94 = f32[4,1536]{1,0:T(4,128)S(1)} fusion(f32[4,512,1536]{2,1,0:T(8,128)} %get-tuple-element.201, f32[4,1536]{1,0:T(4,128)S(1)} %select_maximum_fusion.2, pred[1536,512]{0,1:T(8,128)(4,1)S(1)} %broadcast_compare_fusion.3), kind=kLoop, calls=%fused_computation.5.clone.1 | loop fusion | flops 15722496 | bytes 13418496 | tf_op jit(solution)/shard_map/while/body/eval_jaxpr/reduce_sum | solution.py:59
  156.7 1.4 copy-done.1
  158.1 6.0 %fusion.96 = f32[4,1536,64]{1,2,0:T(8,128)} fusion(f32[4,512,1536]{2,1,0:T(8,128)S(1)} %copy-done.1, f32[4,1536]{1,0:T(4,128)S(1)} %select_maximum_fusion.2, pred[1536,512]{0,1:T(8,128)(4,1)S(1)} %broadcast_compare_fusion.3, f32[4,1536,64]{1,2,0:T(8,128)} %get-tuple-element.220, f32[4,1536]{1,0:T(4,128)S(1)} %get-tuple-element.203, pred[]{:T(512)S(6)} %compare.4, ...), kind=kOutput, calls=%fused_computation.8.clone.1 | convolution fusion | flops 419561472 | bytes 16826372 | tf_op jit(solution)/shard_map/while/body/eval_jaxpr/kqj,kjd->kqd/dot_general | solution.py:60
  164.1 0.7 dynamic_slice.33
  166.6 8.1 %fusion.93 = (f32[4,1536]{1,0:T(4,128)S(1)}, f32[4,512,1536]{2,1,0:T(8,128)}) fusion(pred[1536,512]{0,1:T(8,128)(4,1)S(1)} %broadcast_compare_fusion.3, bf16[4,1536,64]{1,2,0:T(8,128)(2,1)} %get-tuple-element.236, bf16[4,2560,64]{1,2,0:T(8,128)(2,1)} %get-tuple-element.235, s32[]{:T(128)S(6)} %select_n.102), kind=kOutput, calls=%fused_computation.3.clone.1 | convolution fusion | flops 412084224 | bytes 14442500 | tf_op jit(solution)/shard_map/while/body/eval_jaxpr/kqd,kjd->kqj/dot_general | solution.py:51
  174.7 6.9 %fusion.94 = f32[4,1536]{1,0:T(4,128)S(1)} fusion(f32[4,512,1536]{2,1,0:T(8,128)} %get-tuple-element.201, f32[4,1536]{1,0:T(4,128)S(1)} %select_maximum_fusion.2, pred[1536,512]{0,1:T(8,128)(4,1)S(1)} %broadcast_compare_fusion.3), kind=kLoop, calls=%fused_computation.5.clone.1 | loop fusion | flops 15722496 | bytes 13418496 | tf_op jit(solution)/shard_map/while/body/eval_jaxpr/reduce_sum | solution.py:59
  181.6 1.4 copy-done.1
  182.9 6.0 %fusion.96 = f32[4,1536,64]{1,2,0:T(8,128)} fusion(f32[4,512,1536]{2,1,0:T(8,128)S(1)} %copy-done.1, f32[4,1536]{1,0:T(4,128)S(1)} %select_maximum_fusion.2, pred[1536,512]{0,1:T(8,128)(4,1)S(1)} %broadcast_compare_fusion.3, f32[4,1536,64]{1,2,0:T(8,128)} %get-tuple-element.220, f32[4,1536]{1,0:T(4,128)S(1)} %get-tuple-element.203, pred[]{:T(512)S(6)} %compare.4, ...), kind=kOutput, calls=%fused_computation.8.clone.1 | convolution fusion | flops 419561472 | bytes 16826372 | tf_op jit(solution)/shard_map/while/body/eval_jaxpr/kqj,kjd->kqd/dot_general | solution.py:60
  188.9 1.5 divide_convert_fusion
  190.4 1.5 copy.54
  191.9 1.8 convert_element_type.91
  194.2 2.6 convolution_convert_fusion
  198.6 1.2 reduce-window.6
  200.4 22.6 %reduce-scatter.2.cloned.1.call-done = bf16[512,768]{1,0:T(8,128)(2,1)} async-done(((bf16[512,1536]{1,0:T(8,128)(2,1)}), bf16[512,768]{1,0:T(8,128)(2,1)}) %reduce-scatter.2.cloned.1.call-update) | async-done | bytes 786448 | tf_op jit(solution)/shard_map/reduce_scatter | solution.py:136
  223.1 1.5 fusion.28
  224.5 5.2 %psum.7 = f32[512]{0:T(512)S(1)} all-reduce(f32[512]{0:T(512)S(1)} %fusion.28), channel_id=1, replica_groups=mesh['req'=16,'ep'=2] {'ep'}, use_global_device_ids=true, to_apply=%region_12.13 | all-reduce | flops 512 | bytes 4096 | tf_op jit(solution)/shard_map/psum | solution.py:145
  229.7 3.2 fusion.40
  232.9 4.6 %all-to-all-start = ((bf16[4,192,768]{2,1,0:T(8,128)(2,1)}), bf16[4,192,768]{2,1,0:T(8,128)(2,1)}, u32[]{:S(2)}, u32[]{:S(2)}) async-start(bf16[4,192,768]{2,1,0:T(8,128)(2,1)} %fusion.40), calls=%async_computation.1 | async-start | bytes 2359296 | tf_op jit(solution)/shard_map/all_to_all | solution.py:156
  238.0 14.2 %all-to-all-done = bf16[4,192,768]{2,1,0:T(8,128)(2,1)} async-done(((bf16[4,192,768]{2,1,0:T(8,128)(2,1)}), bf16[4,192,768]{2,1,0:T(8,128)(2,1)}, u32[]{:S(2)}, u32[]{:S(2)}) %all-to-all-start) | async-done | bytes 1179680 | tf_op jit(solution)/shard_map/all_to_all | solution.py:156
  252.2 2.4 copy.61
  254.6 3.9 %fusion.68 = f32[2,192,512]{2,1,0:T(8,128)} fusion(bf16[2,192,1536]{2,1,0:T(8,128)(2,1)} %bitcast.104, bf16[2,1536,512]{2,1,0:T(8,128)(2,1)} %all-gather.6.cloned.1.call-done), kind=kOutput, calls=%fused_computation.100 | convolution fusion | flops 603979776 | bytes 5111808 | tf_op jit(solution)/shard_map/ecd,edf->ecf/dot_general | solution.py:159
  258.5 32.5 %all-gather.10.cloned.1.call-done = bf16[2,512,1536]{2,1,0:T(8,128)(2,1)} async-done(((bf16[2,32,1536]{2,1,0:T(8,128)(2,1)}), bf16[2,512,1536]{2,1,0:T(8,128)(2,1)}) %all-gather.10.cloned.1.call-update) | async-done | bytes 3145744 | tf_op jit(solution)/shard_map/all_gather | solution.py:176
  291.0 46.1 %all-gather.8.cloned.1.call-done = bf16[2,1536,512]{2,1,0:T(8,128)(2,1)} async-done(((bf16[2,96,512]{2,1,0:T(8,128)(2,1)}), bf16[2,1536,512]{2,1,0:T(8,128)(2,1)}) %all-gather.8.cloned.1.call-update) | async-done | bytes 3145744 | tf_op jit(solution)/shard_map/all_gather | solution.py:168
  337.2 5.9 %fusion.27 = bf16[2,192,1536]{2,1,0:T(8,128)(2,1)} fusion(bf16[2,512,1536]{2,1,0:T(8,128)(2,1)} %all-gather.10.cloned.1.call-done, f32[2,192]{1,0:T(2,128)S(1)} %constant_dynamic-slice_fusion, bf16[2,192,1536]{2,1,0:T(8,128)(2,1)} %bitcast.105, bf16[2,1536,512]{2,1,0:T(8,128)(2,1)} %all-gather.8.cloned.1.call-done, f32[2,192,512]{2,1,0:T(8,128)} %fusion.68), kind=kOutput, calls=%fused_computation.39 | convolution fusion | flops 1210318848 | bytes 9438720 | tf_op jit(solution)/shard_map/ecf,efd->ecd/dot_general | solution.py:173
  343.1 4.8 %copy.57 = bf16[2,192,1536]{1,0,2:T(2,128)(2,1)} copy(bf16[2,192,1536]{2,1,0:T(8,128)(2,1)} %fusion.27) | data formatting | bytes 2359296 | tf_op jit(solution)/shard_map/convert_element_type | solution.py:179
  347.9 25.2 %all_to_all.36 = bf16[2,192,1536]{1,0,2:T(2,128)(2,1)} all-to-all(bf16[2,192,1536]{1,0,2:T(2,128)(2,1)} %copy.57), channel_id=1, replica_groups=mesh['req'=16,'ep'=2] {'ep'}, dimensions={2} | all-to-all | bytes 2359296 | tf_op jit(solution)/shard_map/all_to_all | solution.py:180
  373.1 4.9 %copy.58 = bf16[2,192,2,768]{3,1,0,2:T(8,128)(2,1)} copy(bf16[2,192,2,768]{1,0,3,2:T(2,128)(2,1)} %bitcast.101) | data formatting | bytes 2359296 | tf_op jit(solution)/shard_map/all_to_all | solution.py:180
  378.0 2.5 bitcast_reduce_fusion
  380.8 0.9 copy-done.3
  381.6 1.2 fusion.44
  (95 shorter events, 11.6 us)
Async XLA Ops:
  8.0 186.2 %copy-start = (bf16[768,1536]{1,0:T(8,128)(2,1)S(1)}, bf16[768,1536]{1,0:T(8,128)(2,1)}, u32[]{:S(2)}) copy-start(bf16[768,1536]{1,0:T(8,128)(2,1)} %param.30) | copy-start | bytes 7077892
  8.0 33.8 %all-gather.12.cloned.1.call-start = ((), (), s32[]{:S(2)}) async-start(), calls=%async_computation.7 | async-start | bytes 2359296 | tf_op jit(solution)/shard_map/all_gather | solution.py:108
  8.1 2.6 copy-start.5
  10.7 1.2 copy-start.11
  10.7 1.8 copy-start.12
  11.8 32.0 %copy-start.10 = (f32[1536]{0:T(1024)S(1)}, f32[1536]{0:T(1024)}, u32[]{:S(2)}) copy-start(f32[1536]{0:T(1024)} %param.25) | copy-start | bytes 18436
  11.8 211.3 %reduce-scatter.2.cloned.1.call-start = ((), (), s32[]{:S(2)}) async-start(), calls=%async_computation.3 | async-start | bytes 2359296 | tf_op jit(solution)/shard_map/reduce_scatter | solution.py:136
  41.8 1.9 copy-start.4
  43.8 2.2 copy-start.9
  75.6 8.3 %copy-start.1 = (f32[4,512,1536]{2,1,0:T(8,128)S(1)}, f32[4,512,1536]{2,1,0:T(8,128)}, u32[]{:S(2)}) copy-start(f32[4,512,1536]{2,1,0:T(8,128)} %get-tuple-element.201) | copy-start | bytes 37748740 | tf_op jit(solution)/shard_map/while
  100.1 8.3 %copy-start.1 = (f32[4,512,1536]{2,1,0:T(8,128)S(1)}, f32[4,512,1536]{2,1,0:T(8,128)}, u32[]{:S(2)}) copy-start(f32[4,512,1536]{2,1,0:T(8,128)} %get-tuple-element.201) | copy-start | bytes 37748740 | tf_op jit(solution)/shard_map/while
  125.0 8.3 %copy-start.1 = (f32[4,512,1536]{2,1,0:T(8,128)S(1)}, f32[4,512,1536]{2,1,0:T(8,128)}, u32[]{:S(2)}) copy-start(f32[4,512,1536]{2,1,0:T(8,128)} %get-tuple-element.201) | copy-start | bytes 37748740 | tf_op jit(solution)/shard_map/while
  149.8 8.3 %copy-start.1 = (f32[4,512,1536]{2,1,0:T(8,128)S(1)}, f32[4,512,1536]{2,1,0:T(8,128)}, u32[]{:S(2)}) copy-start(f32[4,512,1536]{2,1,0:T(8,128)} %get-tuple-element.201) | copy-start | bytes 37748740 | tf_op jit(solution)/shard_map/while
  174.7 8.3 %copy-start.1 = (f32[4,512,1536]{2,1,0:T(8,128)S(1)}, f32[4,512,1536]{2,1,0:T(8,128)}, u32[]{:S(2)}) copy-start(f32[4,512,1536]{2,1,0:T(8,128)} %get-tuple-element.201) | copy-start | bytes 37748740 | tf_op jit(solution)/shard_map/while
  196.8 1.8 copy-start.6
  196.8 3.5 copy-start.8
  196.8 26.3 %copy-start.2 = (bf16[1,512,768]{2,1,0:T(8,128)(2,1)S(1)}, bf16[1,512,768]{2,1,0:T(8,128)(2,1)}, u32[]{:S(2)}) copy-start(bf16[1,512,768]{2,1,0:T(8,128)(2,1)} %param.18) | copy-start | bytes 2359300
  196.8 57.7 %all-gather.6.cloned.1.call-start = ((), (), s32[]{:S(2)}) async-start(), calls=%async_computation.4 | async-start | bytes 3342336 | tf_op jit(solution)/shard_map/all_gather | solution.py:162
  197.4 93.6 %all-gather.10.cloned.1.call-start = ((), (), s32[]{:S(2)}) async-start(), calls=%async_computation.6 | async-start | bytes 3342336 | tf_op jit(solution)/shard_map/all_gather | solution.py:176
  198.0 139.2 %all-gather.8.cloned.1.call-start = ((), (), s32[]{:S(2)}) async-start(), calls=%async_computation.5 | async-start | bytes 3342336 | tf_op jit(solution)/shard_map/all_gather | solution.py:168
  232.9 4.6 %copy-start.7 = (f32[1,512,8]{1,2,0:T(8,128)S(1)}, f32[1,512,8]{1,2,0:T(8,128)}, u32[]{:S(2)}) copy-start(f32[1,512,8]{1,2,0:T(8,128)} %param.24) | copy-start | bytes 49156
  232.9 19.2 %all-to-all-start = ((bf16[4,192,768]{2,1,0:T(8,128)(2,1)}), bf16[4,192,768]{2,1,0:T(8,128)(2,1)}, u32[]{:S(2)}, u32[]{:S(2)}) async-start(bf16[4,192,768]{2,1,0:T(8,128)(2,1)} %fusion.40), calls=%async_computation.1 | async-start | bytes 2359296 | tf_op jit(solution)/shard_map/all_to_all | solution.py:156
  380.5 1.1 copy-start.3
Sparse Core Ops, SparseCore 0:
  11.9 29.8 all-gather.11
  197.0 26.0 reduce-scatter.1
Sparse Core Ops, SparseCore 1:
  199.6 45.5 all-gather.5
  247.3 43.7 all-gather.9
  293.5 43.7 all-gather.7
where the time goes:
time: 392 us; the launch traced here: 390 us
  waiting for transfers between devices  142 us (36%)
  matrix products  93.9 us (24%)
  other arithmetic  54.2 us (14%)
  local copies, waits for them, and re-layouts  43.3 us (11%)
  blocking collectives  30.4 us (8%)
  between operations  17.8 us (5%)
  starting transfers between devices  4.8 us (1%)
    all_gather x1, waiting for transfers between devices, on_device(): lax.all_gather(expert_up, 'req', axis=1, tiled=True)  46.1 us
    dot_general x5, matrix products, visit(): jnp.einsum('kqd,kjd->kqj', query, key_block, preferred_element_type=jnp.f...  40.3 us
    reduce_sum x5, other arithmetic, visit(): total = total * correction + jnp.sum(probs, -1)  34.3 us
    all_gather x1, waiting for transfers between devices, on_device(): lax.all_gather(expert_down, 'req', axis=1, tiled=True)  32.5 us
    dot_general x5, matrix products, visit(): jnp.einsum('kqj,kjd->kqd', probs.astype(jnp.bfloat16), value_block, prefe...  29.5 us
    all_to_all x1, blocking collectives, on_device(): lax.all_to_all(contrib, 'ep', split_axis=2, concat_axis=0, tiled=True)  25.2 us
    all_gather x1, waiting for transfers between devices, on_device(): rows_whole = lax.all_gather(own_rows, 'ep', axis=1, tiled=True)  25.2 us
    reduce_scatter x1, waiting for transfers between devices, on_device(): lax.psum_scatter(partial_value.astype(jnp.bfloat16), 'ep', scatter_dimens...  22.6 us
  transfers between devices with their start and end apart: 6, of which 5 were waited for; matrix products, arithmetic and copies ran while one was open for 4% of the time, Pallas kernels for 0%

commit v1 on v0

--- a/solution.py
+++ b/solution.py
@@ -162,12 +162,38 @@
         lax.all_gather(expert_gate, "req", axis=1, tiled=True),
         preferred_element_type=jnp.float32,
     )
-    up_next = jnp.einsum(
+    size, here, rows = (lax.axis_size("req"), lax.axis_index("req"), expert_up.shape[1])
+    right = [(i, (i + 1) % size) for i in range(size)]
+    left = [(i, (i - 1) % size) for i in range(size)]
+    half_2 = size // 2
+    from_left = from_right = expert_up
+    total_2 = jnp.einsum(
         "ecd,edf->ecf",
-        columns,
-        lax.all_gather(expert_up, "req", axis=1, tiled=True),
+        lax.dynamic_slice_in_dim(columns, here * rows, expert_up.shape[1], axis=2),
+        expert_up,
         preferred_element_type=jnp.float32,
     )
+    for lap in range(1, half_2 + 1):
+        from_left = lax.ppermute(from_left, "req", right)
+        if lap < size - half_2:
+            from_right = lax.ppermute(from_right, "req", left)
+            total_2 = total_2 + jnp.einsum(
+                "ecd,edf->ecf",
+                lax.dynamic_slice_in_dim(
+                    columns, (here + lap) % size * rows, from_right.shape[1], axis=2
+                ),
+                from_right,
+                preferred_element_type=jnp.float32,
+            )
+        total_2 = total_2 + jnp.einsum(
+            "ecd,edf->ecf",
+            lax.dynamic_slice_in_dim(
+                columns, (here - lap) % size * rows, from_left.shape[1], axis=2
+            ),
+            from_left,
+            preferred_element_type=jnp.float32,
+        )
+    up_next = total_2
     hidden_act = (jax.nn.silu(gate_next) * up_next).astype(jnp.bfloat16)
     columns = hidden_act
     output = jnp.einsum(

time: 392 us -> 349 us (0.89)
  waiting for transfers between devices: 142 us -> 48.3 us
  starting transfers between devices: 4.8 us -> 35.2 us
  matrix products: 93.9 us -> 107 us
  other arithmetic: 54.2 us -> 59.8 us
    all_gather x1 -> x0, waiting for transfers between devices: 46.1 us -> none  [on_device(): lax.all_gather(expert_up, 'req', axis=1, tiled=True)]
    ppermute x0 -> x15, starting transfers between devices: none -> 31.4 us  [the longest x7 31.4 us: on_device(): from_right = lax.ppermute(from_right, 'req', left)]
    all_gather x1, waiting for transfers between devices: 32.5 us -> 2.02 us  [on_device(): lax.all_gather(expert_down, 'req', axis=1, tiled=True)]
    reduce_scatter x1, waiting for transfers between devices: 22.6 us -> 0.01 us  [on_device(): lax.psum_scatter(partial_value.astype(jnp.bfloat16), 'ep', scatter_dimens...]
    ppermute x0 -> x15, waiting for transfers between devices: none -> 20.6 us  [the longest x7 15.5 us: on_device(): from_right = lax.ppermute(from_right, 'req', left)]
    dot_general x0 -> x15, matrix products: none -> 16.8 us  [the longest x7 8.72 us: on_device(): jnp.einsum('ecd,edf->ecf', lax.dynamic_slice_in_dim(columns, (here + lap)...]
    all_to_all x1, waiting for transfers between devices: 14.2 us -> 0.01 us  [on_device(): lax.all_to_all(buffers, 'ep', split_axis=0, concat_axis=2, tiled=True)]
  transfers between devices with their start and end apart: 6 -> 20, of which waited for: 5 -> 8; matrix products, arithmetic and copies ran while one was open for 4% -> 11% of each run, Pallas kernels for 0% -> 0%
where the time goes in v1:
time: 349 us; the launch traced here: 347 us
  matrix products  107 us (31%)
  other arithmetic  59.8 us (17%)
  waiting for transfers between devices  48.3 us (14%)
  local copies, waits for them, and re-layouts  44.8 us (13%)
  starting transfers between devices  35.2 us (10%)
  blocking collectives  30.2 us (9%)
  between operations  17.9 us (5%)
    dot_general x5, matrix products, visit(): jnp.einsum('kqd,kjd->kqj', query, key_block, preferred_element_type=jnp.f...  40 us
    reduce_sum x5, other arithmetic, visit(): total = total * correction + jnp.sum(probs, -1)  34.3 us
    ppermute x7, starting transfers between devices, on_device(): from_right = lax.ppermute(from_right, 'req', left)  31.4 us
    dot_general x5, matrix products, visit(): jnp.einsum('kqj,kjd->kqd', probs.astype(jnp.bfloat16), value_block, prefe...  29.4 us
    all_to_all x1, blocking collectives, on_device(): lax.all_to_all(contrib, 'ep', split_axis=2, concat_axis=0, tiled=True)  25.2 us
    all_gather x1, waiting for transfers between devices, on_device(): rows_whole = lax.all_gather(own_rows, 'ep', axis=1, tiled=True)  25.1 us
    ppermute x7, waiting for transfers between devices, on_device(): from_right = lax.ppermute(from_right, 'req', left)  15.5 us
    dot_general x7, matrix products, on_device(): jnp.einsum('ecd,edf->ecf', lax.dynamic_slice_in_dim(columns, (here + lap)...  8.72 us
  transfers between devices with their start and end apart: 20, of which 8 were waited for; matrix products, arithmetic and copies ran while one was open for 11% of the time, Pallas kernels for 0%

profile of v1, /device:TPU:0, one launch (start us, length us, event | category | flops | bytes accessed | tf_op | source)
XLA Modules:
  0.0 346.7 jit_solution(3558293803725290666)
XLA Ops:
  8.1 2.6 copy.81
  12.5 1.3 fusion.108
  16.7 25.1 %all-gather.9.cloned.1.call-done = bf16[1,512,1536]{2,1,0:T(8,128)(2,1)} async-done(((bf16[1,512,768]{2,1,0:T(8,128)(2,1)}), bf16[1,512,1536]{2,1,0:T(8,128)(2,1)}) %all-gather.9.cloned.1.call-update) | async-done | bytes 1572880 | tf_op jit(solution)/shard_map/all_gather | solution.py:108
  41.8 1.9 fusion.24
  43.8 2.1 fusion.114
  46.0 1.6 fusion.112
  52.1 1.6 pad_maximum_fusion
  54.8 4.0 %dynamic_update_slice.6 = bf16[4,2560,64]{1,2,0:T(8,128)(2,1)} dynamic-update-slice(bf16[4,2560,64]{1,2,0:T(8,128)(2,1)} %bitcast.133, bf16[4,512,64]{1,2,0:T(8,128)(2,1)S(1)} %pad_maximum_fusion.1, s32[]{:T(128)} %constant.145.clone.1, s32[]{:T(128)S(6)} %select_n.156, s32[]{:T(128)} %constant.145.clone.1) | dynamic-update-slice | bytes 524292 | tf_op jit(solution)/shard_map/dynamic_update_slice | solution.py:126
  58.8 2.4 convolution_convert_fusion.1
  61.2 3.8 %dynamic_update_slice.7 = bf16[4,2560,64]{1,2,0:T(8,128)(2,1)} dynamic-update-slice(bf16[4,2560,64]{1,2,0:T(8,128)(2,1)} %bitcast.139, bf16[4,512,64]{1,2,0:T(8,128)(2,1)S(1)} %bitcast.143, s32[]{:T(128)} %constant.145.clone.1, s32[]{:T(128)S(6)} %select_n.156, s32[]{:T(128)} %constant.145.clone.1) | dynamic-update-slice | bytes 524292 | tf_op jit(solution)/shard_map/dynamic_update_slice | solution.py:127
  65.0 123.1 %while.15 = (s32[]{:T(128)}, f32[4,1536]{1,0:T(4,128)S(1)}, f32[4,1536]{1,0:T(4,128)S(1)}, f32[4,1536,64]{1,2,0:T(8,128)}, s32[5]{0:T(128)S(1)}, /*index=5*/bf16...) while((s32[]{:T(128)}, f32[4,1536]{1,0:T(4,128)S(1)}, ...), condition=%wide.region_6.7_spmd.clone, body=%wide.region_3.6_spmd.clone.sunk | while | flops 848208896 | bytes 96092400 | solution.py:73
  67.4 8.0 %fusion.155 = (f32[4,1536]{1,0:T(4,128)S(1)}, f32[4,512,1536]{2,1,0:T(8,128)}) fusion(pred[1536,512]{0,1:T(8,128)(4,1)S(1)} %broadcast_compare_fusion.3, bf16[4,1536,64]{1,2,0:T(8,128)(2,1)} %get-tuple-element.236, bf16[4,2560,64]{1,2,0:T(8,128)(2,1)} %get-tuple-element.235, s32[]{:T(128)S(6)} %select_n.243), kind=kOutput, calls=%fused_computation.3.clone.1 | convolution fusion | flops 412084224 | bytes 14442500 | tf_op jit(solution)/shard_map/while/body/eval_jaxpr/kqd,kjd->kqj/dot_general | solution.py:51
  75.4 6.9 %fusion.156 = f32[4,1536]{1,0:T(4,128)S(1)} fusion(f32[4,512,1536]{2,1,0:T(8,128)} %get-tuple-element.201, f32[4,1536]{1,0:T(4,128)S(1)} %select_maximum_fusion.2, pred[1536,512]{0,1:T(8,128)(4,1)S(1)} %broadcast_compare_fusion.3), kind=kLoop, calls=%fused_computation.5.clone.1 | loop fusion | flops 15722496 | bytes 13418496 | tf_op jit(solution)/shard_map/while/body/eval_jaxpr/reduce_sum | solution.py:59
  82.3 1.4 copy-done.1
  83.7 5.7 %fusion.158 = f32[4,1536,64]{1,2,0:T(8,128)} fusion(f32[4,512,1536]{2,1,0:T(8,128)S(1)} %copy-done.1, f32[4,1536]{1,0:T(4,128)S(1)} %select_maximum_fusion.2, pred[1536,512]{0,1:T(8,128)(4,1)S(1)} %broadcast_compare_fusion.3, f32[4,1536,64]{1,2,0:T(8,128)} %get-tuple-element.220, f32[4,1536]{1,0:T(4,128)S(1)} %get-tuple-element.203, ...), kind=kOutput, calls=%fused_computation.8.clone.1 | convolution fusion | flops 419561472 | bytes 16826372 | tf_op jit(solution)/shard_map/while/body/eval_jaxpr/kqj,kjd->kqd/dot_general | solution.py:60
  91.8 8.0 %fusion.155 = (f32[4,1536]{1,0:T(4,128)S(1)}, f32[4,512,1536]{2,1,0:T(8,128)}) fusion(pred[1536,512]{0,1:T(8,128)(4,1)S(1)} %broadcast_compare_fusion.3, bf16[4,1536,64]{1,2,0:T(8,128)(2,1)} %get-tuple-element.236, bf16[4,2560,64]{1,2,0:T(8,128)(2,1)} %get-tuple-element.235, s32[]{:T(128)S(6)} %select_n.243), kind=kOutput, calls=%fused_computation.3.clone.1 | convolution fusion | flops 412084224 | bytes 14442500 | tf_op jit(solution)/shard_map/while/body/eval_jaxpr/kqd,kjd->kqj/dot_general | solution.py:51
  99.8 6.9 %fusion.156 = f32[4,1536]{1,0:T(4,128)S(1)} fusion(f32[4,512,1536]{2,1,0:T(8,128)} %get-tuple-element.201, f32[4,1536]{1,0:T(4,128)S(1)} %select_maximum_fusion.2, pred[1536,512]{0,1:T(8,128)(4,1)S(1)} %broadcast_compare_fusion.3), kind=kLoop, calls=%fused_computation.5.clone.1 | loop fusion | flops 15722496 | bytes 13418496 | tf_op jit(solution)/shard_map/while/body/eval_jaxpr/reduce_sum | solution.py:59
  106.7 1.4 copy-done.1
  108.1 5.9 %fusion.158 = f32[4,1536,64]{1,2,0:T(8,128)} fusion(f32[4,512,1536]{2,1,0:T(8,128)S(1)} %copy-done.1, f32[4,1536]{1,0:T(4,128)S(1)} %select_maximum_fusion.2, pred[1536,512]{0,1:T(8,128)(4,1)S(1)} %broadcast_compare_fusion.3, f32[4,1536,64]{1,2,0:T(8,128)} %get-tuple-element.220, f32[4,1536]{1,0:T(4,128)S(1)} %get-tuple-element.203, ...), kind=kOutput, calls=%fused_computation.8.clone.1 | convolution fusion | flops 419561472 | bytes 16826372 | tf_op jit(solution)/shard_map/while/body/eval_jaxpr/kqj,kjd->kqd/dot_general | solution.py:60
  116.5 8.0 %fusion.155 = (f32[4,1536]{1,0:T(4,128)S(1)}, f32[4,512,1536]{2,1,0:T(8,128)}) fusion(pred[1536,512]{0,1:T(8,128)(4,1)S(1)} %broadcast_compare_fusion.3, bf16[4,1536,64]{1,2,0:T(8,128)(2,1)} %get-tuple-element.236, bf16[4,2560,64]{1,2,0:T(8,128)(2,1)} %get-tuple-element.235, s32[]{:T(128)S(6)} %select_n.243), kind=kOutput, calls=%fused_computation.3.clone.1 | convolution fusion | flops 412084224 | bytes 14442500 | tf_op jit(solution)/shard_map/while/body/eval_jaxpr/kqd,kjd->kqj/dot_general | solution.py:51
  124.5 6.9 %fusion.156 = f32[4,1536]{1,0:T(4,128)S(1)} fusion(f32[4,512,1536]{2,1,0:T(8,128)} %get-tuple-element.201, f32[4,1536]{1,0:T(4,128)S(1)} %select_maximum_fusion.2, pred[1536,512]{0,1:T(8,128)(4,1)S(1)} %broadcast_compare_fusion.3), kind=kLoop, calls=%fused_computation.5.clone.1 | loop fusion | flops 15722496 | bytes 13418496 | tf_op jit(solution)/shard_map/while/body/eval_jaxpr/reduce_sum | solution.py:59
  131.4 1.4 copy-done.1
  132.8 5.9 %fusion.158 = f32[4,1536,64]{1,2,0:T(8,128)} fusion(f32[4,512,1536]{2,1,0:T(8,128)S(1)} %copy-done.1, f32[4,1536]{1,0:T(4,128)S(1)} %select_maximum_fusion.2, pred[1536,512]{0,1:T(8,128)(4,1)S(1)} %broadcast_compare_fusion.3, f32[4,1536,64]{1,2,0:T(8,128)} %get-tuple-element.220, f32[4,1536]{1,0:T(4,128)S(1)} %get-tuple-element.203, ...), kind=kOutput, calls=%fused_computation.8.clone.1 | convolution fusion | flops 419561472 | bytes 16826372 | tf_op jit(solution)/shard_map/while/body/eval_jaxpr/kqj,kjd->kqd/dot_general | solution.py:60
  141.2 8.0 %fusion.155 = (f32[4,1536]{1,0:T(4,128)S(1)}, f32[4,512,1536]{2,1,0:T(8,128)}) fusion(pred[1536,512]{0,1:T(8,128)(4,1)S(1)} %broadcast_compare_fusion.3, bf16[4,1536,64]{1,2,0:T(8,128)(2,1)} %get-tuple-element.236, bf16[4,2560,64]{1,2,0:T(8,128)(2,1)} %get-tuple-element.235, s32[]{:T(128)S(6)} %select_n.243), kind=kOutput, calls=%fused_computation.3.clone.1 | convolution fusion | flops 412084224 | bytes 14442500 | tf_op jit(solution)/shard_map/while/body/eval_jaxpr/kqd,kjd->kqj/dot_general | solution.py:51
  149.2 6.9 %fusion.156 = f32[4,1536]{1,0:T(4,128)S(1)} fusion(f32[4,512,1536]{2,1,0:T(8,128)} %get-tuple-element.201, f32[4,1536]{1,0:T(4,128)S(1)} %select_maximum_fusion.2, pred[1536,512]{0,1:T(8,128)(4,1)S(1)} %broadcast_compare_fusion.3), kind=kLoop, calls=%fused_computation.5.clone.1 | loop fusion | flops 15722496 | bytes 13418496 | tf_op jit(solution)/shard_map/while/body/eval_jaxpr/reduce_sum | solution.py:59
  156.1 1.4 copy-done.1
  157.4 5.9 %fusion.158 = f32[4,1536,64]{1,2,0:T(8,128)} fusion(f32[4,512,1536]{2,1,0:T(8,128)S(1)} %copy-done.1, f32[4,1536]{1,0:T(4,128)S(1)} %select_maximum_fusion.2, pred[1536,512]{0,1:T(8,128)(4,1)S(1)} %broadcast_compare_fusion.3, f32[4,1536,64]{1,2,0:T(8,128)} %get-tuple-element.220, f32[4,1536]{1,0:T(4,128)S(1)} %get-tuple-element.203, ...), kind=kOutput, calls=%fused_computation.8.clone.1 | convolution fusion | flops 419561472 | bytes 16826372 | tf_op jit(solution)/shard_map/while/body/eval_jaxpr/kqj,kjd->kqd/dot_general | solution.py:60
  165.8 8.0 %fusion.155 = (f32[4,1536]{1,0:T(4,128)S(1)}, f32[4,512,1536]{2,1,0:T(8,128)}) fusion(pred[1536,512]{0,1:T(8,128)(4,1)S(1)} %broadcast_compare_fusion.3, bf16[4,1536,64]{1,2,0:T(8,128)(2,1)} %get-tuple-element.236, bf16[4,2560,64]{1,2,0:T(8,128)(2,1)} %get-tuple-element.235, s32[]{:T(128)S(6)} %select_n.243), kind=kOutput, calls=%fused_computation.3.clone.1 | convolution fusion | flops 412084224 | bytes 14442500 | tf_op jit(solution)/shard_map/while/body/eval_jaxpr/kqd,kjd->kqj/dot_general | solution.py:51
  173.9 6.9 %fusion.156 = f32[4,1536]{1,0:T(4,128)S(1)} fusion(f32[4,512,1536]{2,1,0:T(8,128)} %get-tuple-element.201, f32[4,1536]{1,0:T(4,128)S(1)} %select_maximum_fusion.2, pred[1536,512]{0,1:T(8,128)(4,1)S(1)} %broadcast_compare_fusion.3), kind=kLoop, calls=%fused_computation.5.clone.1 | loop fusion | flops 15722496 | bytes 13418496 | tf_op jit(solution)/shard_map/while/body/eval_jaxpr/reduce_sum | solution.py:59
  180.8 1.4 copy-done.1
  182.1 5.9 %fusion.158 = f32[4,1536,64]{1,2,0:T(8,128)} fusion(f32[4,512,1536]{2,1,0:T(8,128)S(1)} %copy-done.1, f32[4,1536]{1,0:T(4,128)S(1)} %select_maximum_fusion.2, pred[1536,512]{0,1:T(8,128)(4,1)S(1)} %broadcast_compare_fusion.3, f32[4,1536,64]{1,2,0:T(8,128)} %get-tuple-element.220, f32[4,1536]{1,0:T(4,128)S(1)} %get-tuple-element.203, ...), kind=kOutput, calls=%fused_computation.8.clone.1 | convolution fusion | flops 419561472 | bytes 16826372 | tf_op jit(solution)/shard_map/while/body/eval_jaxpr/kqj,kjd->kqd/dot_general | solution.py:60
  188.1 1.5 divide_convert_fusion
  189.6 1.5 copy.54
  191.1 1.8 convert_element_type.91
  193.4 2.6 convolution_convert_fusion
  196.9 4.4 %collective-permute-start = (bf16[2,96,512]{2,1,0:T(8,128)(2,1)S(1)}, bf16[2,96,512]{2,1,0:T(8,128)(2,1)}, u32[]{:S(2)}, u32[]{:S(2)}) collective-permute-start(bf16[2,96,512]{2,1,0:T(8,128)(2,1)S(1)} %copy-done.10), channel_id=1, source_target_pairs={{0,30},{2,0},{4,2},{6,4},{8,6},{10,8},{12,10},{14,12},{16,14},{18,... | collective-permute-start | bytes 589832 | tf_op jit(solution)/shard_map/ppermute | solution.py:179
  201.4 3.4 collective-permute-done.1
  206.2 2.3 reduce-window.6
  209.2 1.4 reduce-window.9
  210.6 4.4 %collective-permute-start.2 = (bf16[2,96,512]{2,1,0:T(8,128)(2,1)}, bf16[2,96,512]{2,1,0:T(8,128)(2,1)S(1)}, u32[]{:S(2)}, u32[]{:S(2)}) collective-permute-start(bf16[2,96,512]{2,1,0:T(8,128)(2,1)} %collective-permute-done), channel_id=1, source_target_pairs={{0,30},{2,0},{4,2},{6,4},{8,6},{10,8},{12,10},{14,12},{16,14},{18,... | collective-permute-start | bytes 589832 | tf_op jit(solution)/shard_map/ppermute | solution.py:179
  215.7 1.4 dynamic_slice.64
  217.1 2.6 collective-permute-done.2
  219.7 4.6 %collective-permute-start.4 = (bf16[2,96,512]{2,1,0:T(8,128)(2,1)S(1)}, bf16[2,96,512]{2,1,0:T(8,128)(2,1)}, u32[]{:S(2)}, u32[]{:S(2)}) collective-permute-start(bf16[2,96,512]{2,1,0:T(8,128)(2,1)S(1)} %collective-permute-done.2), channel_id=1, source_target_pairs={{0,30},{2,0},{4,2},{6,4},{8,6},{10,8},{12,10},{14,12},{16,14},{18,... | collective-permute-start | bytes 589832 | tf_op jit(solution)/shard_map/ppermute | solution.py:179
  224.8 6.2 %collective-permute-done.4 = bf16[2,96,512]{2,1,0:T(8,128)(2,1)} collective-permute-done((bf16[2,96,512]{2,1,0:T(8,128)(2,1)S(1)}, bf16[2,96,512]{2,1,0:T(8,128)(2,1)}, u32[]{:S(2)}, u32[]{:S(2)}) %collective-permute-start.4) | collective-permute-done | bytes 196640 | tf_op jit(solution)/shard_map/ppermute | solution.py:179
  231.0 4.7 %collective-permute-start.6 = (bf16[2,96,512]{2,1,0:T(8,128)(2,1)}, bf16[2,96,512]{2,1,0:T(8,128)(2,1)}, u32[]{:S(2)}, u32[]{:S(2)}) collective-permute-start(bf16[2,96,512]{2,1,0:T(8,128)(2,1)} %collective-permute-done.4), channel_id=1, source_target_pairs={{0,30},{2,0},{4,2},{6,4},{8,6},{10,8},{12,10},{14,12},{16,14},{18,... | collective-permute-start | bytes 589832 | tf_op jit(solution)/shard_map/ppermute | solution.py:179
  235.8 1.5 fusion.28
  237.2 4.9 %psum.7 = f32[512]{0:T(512)S(1)} all-reduce(f32[512]{0:T(512)S(1)} %fusion.28), channel_id=1, replica_groups=mesh['req'=16,'ep'=2] {'ep'}, use_global_device_ids=true, to_apply=%region_12.13 | all-reduce | flops 512 | bytes 4096 | tf_op jit(solution)/shard_map/psum | solution.py:145
  242.2 3.2 fusion.40
  245.5 3.6 %all-to-all-start = ((bf16[4,192,768]{2,1,0:T(8,128)(2,1)}), bf16[4,192,768]{2,1,0:T(8,128)(2,1)S(1)}, u32[]{:S(2)}, u32[]{:S(2)}) async-start(bf16[4,192,768]{2,1,0:T(8,128)(2,1)} %fusion.40), calls=%async_computation.1 | async-start | bytes 2359296 | tf_op jit(solution)/shard_map/all_to_all | solution.py:156
  249.1 3.9 %collective-permute-start.8 = (bf16[2,96,512]{2,1,0:T(8,128)(2,1)}, bf16[2,96,512]{2,1,0:T(8,128)(2,1)}, u32[]{:S(2)}, u32[]{:S(2)}) collective-permute-start(bf16[2,96,512]{2,1,0:T(8,128)(2,1)} %collective-permute-done.6), channel_id=1, source_target_pairs={{0,30},{2,0},{4,2},{6,4},{8,6},{10,8},{12,10},{14,12},{16,14},{18,... | collective-permute-start | bytes 589832 | tf_op jit(solution)/shard_map/ppermute | solution.py:179
  253.7 2.7 collective-permute-done.8
  256.5 4.7 %collective-permute-start.10 = (bf16[2,96,512]{2,1,0:T(8,128)(2,1)}, bf16[2,96,512]{2,1,0:T(8,128)(2,1)}, u32[]{:S(2)}, u32[]{:S(2)}) collective-permute-start(bf16[2,96,512]{2,1,0:T(8,128)(2,1)} %collective-permute-done.8), channel_id=1, source_target_pairs={{0,30},{2,0},{4,2},{6,4},{8,6},{10,8},{12,10},{14,12},{16,14},{18,... | collective-permute-start | bytes 589832 | tf_op jit(solution)/shard_map/ppermute | solution.py:179
  262.3 3.9 %collective-permute-done.10 = bf16[2,96,512]{2,1,0:T(8,128)(2,1)} collective-permute-done((bf16[2,96,512]{2,1,0:T(8,128)(2,1)}, bf16[2,96,512]{2,1,0:T(8,128)(2,1)}, u32[]{:S(2)}, u32[]{:S(2)}) %collective-permute-start.10) | collective-permute-done | bytes 196640 | tf_op jit(solution)/shard_map/ppermute | solution.py:179
  266.2 4.6 %collective-permute-start.12 = (bf16[2,96,512]{2,1,0:T(8,128)(2,1)}, bf16[2,96,512]{2,1,0:T(8,128)(2,1)}, u32[]{:S(2)}, u32[]{:S(2)}) collective-permute-start(bf16[2,96,512]{2,1,0:T(8,128)(2,1)} %collective-permute-done.10), channel_id=1, source_target_pairs={{0,30},{2,0},{4,2},{6,4},{8,6},{10,8},{12,10},{14,12},{16,14},{18,... | collective-permute-start | bytes 589832 | tf_op jit(solution)/shard_map/ppermute | solution.py:179
  270.8 1.7 collective-permute-done.13
  273.6 1.4 copy.61
  280.3 1.3 fusion.71
  289.8 2.1 fusion.44
  291.9 3.6 %fusion.116 = f32[2,192,512]{2,1,0:T(8,128)} fusion(bf16[2,192,1536]{2,1,0:T(8,128)(2,1)S(1)} %bitcast.130, bf16[2,1536,512]{2,1,0:T(8,128)(2,1)} %all-gather.5.cloned.1.call-done), kind=kOutput, calls=%fused_computation.154 | convolution fusion | flops 603979776 | bytes 5111808 | tf_op jit(solution)/shard_map/ecd,edf->ecf/dot_general | solution.py:159
  295.5 2.0 all-gather.7.cloned.1.call-done
  297.5 4.5 %fusion.27 = bf16[2,192,1536]{2,1,0:T(8,128)(2,1)} fusion(bf16[2,512,1536]{2,1,0:T(8,128)(2,1)} %all-gather.7.cloned.1.call-done, f32[2,192,512]{2,1,0:T(8,128)} %fusion.44, bf16[2,96,512]{2,1,0:T(8,128)(2,1)} %collective-permute-done.14, f32[2,192]{1,0:T(2,128)S(1)} %constant_dynamic-slice_fusion, f32[2,192,512]{2,1,0:T(8,128)} %fusion.116, ...), kind=kOutput, calls=%fused_computation.39 | convolution fusion | flops 644284416 | bytes 6195204 | tf_op jit(solution)/shard_map/ecf,efd->ecd/dot_general | solution.py:199
  302.0 4.8 %copy.57 = bf16[2,192,1536]{1,0,2:T(2,128)(2,1)} copy(bf16[2,192,1536]{2,1,0:T(8,128)(2,1)} %fusion.27) | data formatting | bytes 2359296 | tf_op jit(solution)/shard_map/convert_element_type | solution.py:205
  306.9 25.2 %all_to_all.36 = bf16[2,192,1536]{1,0,2:T(2,128)(2,1)} all-to-all(bf16[2,192,1536]{1,0,2:T(2,128)(2,1)} %copy.57), channel_id=1, replica_groups=mesh['req'=16,'ep'=2] {'ep'}, dimensions={2} | all-to-all | bytes 2359296 | tf_op jit(solution)/shard_map/all_to_all | solution.py:206
  332.1 3.6 %copy.58 = bf16[2,192,2,768]{3,1,0,2:T(8,128)(2,1)S(1)} copy(bf16[2,192,2,768]{1,0,3,2:T(2,128)(2,1)} %bitcast.132) | data formatting | bytes 2359296 | tf_op jit(solution)/shard_map/all_to_all | solution.py:206
  (155 shorter events, 42.4 us)
Async XLA Ops:
  8.0 185.4 %copy-start = (bf16[768,1536]{1,0:T(8,128)(2,1)S(1)}, bf16[768,1536]{1,0:T(8,128)(2,1)}, u32[]{:S(2)}) copy-start(bf16[768,1536]{1,0:T(8,128)(2,1)} %param.30) | copy-start | bytes 7077892
  8.0 33.8 %all-gather.9.cloned.1.call-start = ((), (), s32[]{:S(2)}) async-start(), calls=%async_computation.6 | async-start | bytes 2359296 | tf_op jit(solution)/shard_map/all_gather | solution.py:108
  8.1 2.6 copy-start.7
  10.7 1.2 copy-start.20
  10.7 1.8 copy-start.21
  11.8 32.0 %copy-start.19 = (f32[1536]{0:T(1024)S(1)}, f32[1536]{0:T(1024)}, u32[]{:S(2)}) copy-start(f32[1536]{0:T(1024)} %param.25) | copy-start | bytes 18436
  11.8 224.0 %reduce-scatter.2.cloned.1.call-start = ((), (), s32[]{:S(2)}) async-start(), calls=%async_computation.3 | async-start | bytes 2359296 | tf_op jit(solution)/shard_map/reduce_scatter | solution.py:136
  41.8 1.9 copy-start.6
  43.8 2.2 copy-start.18
  75.4 8.3 %copy-start.1 = (f32[4,512,1536]{2,1,0:T(8,128)S(1)}, f32[4,512,1536]{2,1,0:T(8,128)}, u32[]{:S(2)}) copy-start(f32[4,512,1536]{2,1,0:T(8,128)} %get-tuple-element.201) | copy-start | bytes 37748740 | tf_op jit(solution)/shard_map/while
  99.8 8.3 %copy-start.1 = (f32[4,512,1536]{2,1,0:T(8,128)S(1)}, f32[4,512,1536]{2,1,0:T(8,128)}, u32[]{:S(2)}) copy-start(f32[4,512,1536]{2,1,0:T(8,128)} %get-tuple-element.201) | copy-start | bytes 37748740 | tf_op jit(solution)/shard_map/while
  124.5 8.3 %copy-start.1 = (f32[4,512,1536]{2,1,0:T(8,128)S(1)}, f32[4,512,1536]{2,1,0:T(8,128)}, u32[]{:S(2)}) copy-start(f32[4,512,1536]{2,1,0:T(8,128)} %get-tuple-element.201) | copy-start | bytes 37748740 | tf_op jit(solution)/shard_map/while
  149.2 8.3 %copy-start.1 = (f32[4,512,1536]{2,1,0:T(8,128)S(1)}, f32[4,512,1536]{2,1,0:T(8,128)}, u32[]{:S(2)}) copy-start(f32[4,512,1536]{2,1,0:T(8,128)} %get-tuple-element.201) | copy-start | bytes 37748740 | tf_op jit(solution)/shard_map/while
  173.8 8.3 %copy-start.1 = (f32[4,512,1536]{2,1,0:T(8,128)S(1)}, f32[4,512,1536]{2,1,0:T(8,128)}, u32[]{:S(2)}) copy-start(f32[4,512,1536]{2,1,0:T(8,128)} %get-tuple-element.201) | copy-start | bytes 37748740 | tf_op jit(solution)/shard_map/while
  196.0 0.9 copy-start.10
  196.0 39.8 %copy-start.2 = (bf16[1,512,768]{2,1,0:T(8,128)(2,1)S(1)}, bf16[1,512,768]{2,1,0:T(8,128)(2,1)}, u32[]{:S(2)}) copy-start(bf16[1,512,768]{2,1,0:T(8,128)(2,1)} %param.18) | copy-start | bytes 2359300
  196.0 96.0 %all-gather.5.cloned.1.call-start = ((), (), s32[]{:S(2)}) async-start(), calls=%async_computation.4 | async-start | bytes 3342336 | tf_op jit(solution)/shard_map/all_gather | solution.py:162
  196.6 101.0 %all-gather.7.cloned.1.call-start = ((), (), s32[]{:S(2)}) async-start(), calls=%async_computation.5 | async-start | bytes 3342336 | tf_op jit(solution)/shard_map/all_gather | solution.py:202
  196.9 7.9 %collective-permute-start.1 = (bf16[2,96,512]{2,1,0:T(8,128)(2,1)S(1)}, bf16[2,96,512]{2,1,0:T(8,128)(2,1)S(1)}, u32[]{:S(2)}, u32[]{:S(2)}) collective-permute-start(bf16[2,96,512]{2,1,0:T(8,128)(2,1)S(1)} %copy-done.10), channel_id=1, source_target_pairs={{0,2},{2,4},{4,6},{6,8},{8,10},{10,12},{12,14},{14,16},{16,18},{18... | collective-permute-start | bytes 589832 | tf_op jit(solution)/shard_map/ppermute | solution.py:177
  196.9 13.7 %collective-permute-start = (bf16[2,96,512]{2,1,0:T(8,128)(2,1)S(1)}, bf16[2,96,512]{2,1,0:T(8,128)(2,1)}, u32[]{:S(2)}, u32[]{:S(2)}) collective-permute-start(bf16[2,96,512]{2,1,0:T(8,128)(2,1)S(1)} %copy-done.10), channel_id=1, source_target_pairs={{0,30},{2,0},{4,2},{6,4},{8,6},{10,8},{12,10},{14,12},{16,14},{18,... | collective-permute-start | bytes 589832 | tf_op jit(solution)/shard_map/ppermute | solution.py:179
  204.8 40.7 %copy-start.12 = (bf16[2,96,512]{2,1,0:T(8,128)(2,1)}, bf16[2,96,512]{2,1,0:T(8,128)(2,1)S(1)}, u32[]{:S(2)}) copy-start(bf16[2,96,512]{2,1,0:T(8,128)(2,1)S(1)} %collective-permute-done.1) | copy-start | bytes 589828
  204.8 10.2 %collective-permute-start.3 = (bf16[2,96,512]{2,1,0:T(8,128)(2,1)S(1)}, bf16[2,96,512]{2,1,0:T(8,128)(2,1)}, u32[]{:S(2)}, u32[]{:S(2)}) collective-permute-start(bf16[2,96,512]{2,1,0:T(8,128)(2,1)S(1)} %collective-permute-done.1), channel_id=1, source_target_pairs={{0,2},{2,4},{4,6},{6,8},{8,10},{10,12},{12,14},{14,16},{16,18},{18... | collective-permute-start | bytes 589832 | tf_op jit(solution)/shard_map/ppermute | solution.py:177
  210.6 9.1 %collective-permute-start.2 = (bf16[2,96,512]{2,1,0:T(8,128)(2,1)}, bf16[2,96,512]{2,1,0:T(8,128)(2,1)S(1)}, u32[]{:S(2)}, u32[]{:S(2)}) collective-permute-start(bf16[2,96,512]{2,1,0:T(8,128)(2,1)} %collective-permute-done), channel_id=1, source_target_pairs={{0,30},{2,0},{4,2},{6,4},{8,6},{10,8},{12,10},{14,12},{16,14},{18,... | collective-permute-start | bytes 589832 | tf_op jit(solution)/shard_map/ppermute | solution.py:179
  215.0 9.3 %collective-permute-start.5 = (bf16[2,96,512]{2,1,0:T(8,128)(2,1)}, bf16[2,96,512]{2,1,0:T(8,128)(2,1)}, u32[]{:S(2)}, u32[]{:S(2)}) collective-permute-start(bf16[2,96,512]{2,1,0:T(8,128)(2,1)} %collective-permute-done.3), channel_id=1, source_target_pairs={{0,2},{2,4},{4,6},{6,8},{8,10},{10,12},{12,14},{14,16},{16,18},{18... | collective-permute-start | bytes 589832 | tf_op jit(solution)/shard_map/ppermute | solution.py:177
  215.7 26.5 %copy-start.15 = (s32[1,4,4,128]{3,1,2,0:T(4,128)}, s32[1,4,4,128]{3,1,2,0:T(4,128)S(1)}, u32[]{:S(2)}) copy-start(s32[1,4,4,128]{3,1,2,0:T(4,128)S(1)} %copy.64) | copy-start | bytes 24580
  219.7 25.8 %copy-start.8 = (bf16[2,96,512]{2,1,0:T(8,128)(2,1)}, bf16[2,96,512]{2,1,0:T(8,128)(2,1)S(1)}, u32[]{:S(2)}) copy-start(bf16[2,96,512]{2,1,0:T(8,128)(2,1)S(1)} %collective-permute-done.2) | copy-start | bytes 589828
  219.7 11.4 %collective-permute-start.4 = (bf16[2,96,512]{2,1,0:T(8,128)(2,1)S(1)}, bf16[2,96,512]{2,1,0:T(8,128)(2,1)}, u32[]{:S(2)}, u32[]{:S(2)}) collective-permute-start(bf16[2,96,512]{2,1,0:T(8,128)(2,1)S(1)} %collective-permute-done.2), channel_id=1, source_target_pairs={{0,30},{2,0},{4,2},{6,4},{8,6},{10,8},{12,10},{14,12},{16,14},{18,... | collective-permute-start | bytes 589832 | tf_op jit(solution)/shard_map/ppermute | solution.py:179
  224.3 11.5 %collective-permute-start.7 = (bf16[2,96,512]{2,1,0:T(8,128)(2,1)}, bf16[2,96,512]{2,1,0:T(8,128)(2,1)}, u32[]{:S(2)}, u32[]{:S(2)}) collective-permute-start(bf16[2,96,512]{2,1,0:T(8,128)(2,1)} %collective-permute-done.5), channel_id=1, source_target_pairs={{0,2},{2,4},{4,6},{6,8},{8,10},{10,12},{12,14},{14,16},{16,18},{18... | collective-permute-start | bytes 589832 | tf_op jit(solution)/shard_map/ppermute | solution.py:177
  231.0 18.0 %collective-permute-start.6 = (bf16[2,96,512]{2,1,0:T(8,128)(2,1)}, bf16[2,96,512]{2,1,0:T(8,128)(2,1)}, u32[]{:S(2)}, u32[]{:S(2)}) collective-permute-start(bf16[2,96,512]{2,1,0:T(8,128)(2,1)} %collective-permute-done.4), channel_id=1, source_target_pairs={{0,30},{2,0},{4,2},{6,4},{8,6},{10,8},{12,10},{14,12},{16,14},{18,... | collective-permute-start | bytes 589832 | tf_op jit(solution)/shard_map/ppermute | solution.py:179
  235.8 17.2 %collective-permute-start.9 = (bf16[2,96,512]{2,1,0:T(8,128)(2,1)}, bf16[2,96,512]{2,1,0:T(8,128)(2,1)}, u32[]{:S(2)}, u32[]{:S(2)}) collective-permute-start(bf16[2,96,512]{2,1,0:T(8,128)(2,1)} %collective-permute-done.7), channel_id=1, source_target_pairs={{0,2},{2,4},{4,6},{6,8},{8,10},{10,12},{12,14},{14,16},{16,18},{18... | collective-permute-start | bytes 589832 | tf_op jit(solution)/shard_map/ppermute | solution.py:177
  245.5 7.5 %copy-start.14 = (s32[1,512,8]{1,2,0:T(8,128)S(1)}, s32[1,512,8]{1,2,0:T(8,128)}, u32[]{:S(2)}) copy-start(s32[1,512,8]{1,2,0:T(8,128)} %param.23) | copy-start | bytes 49156
  245.5 27.1 %all-to-all-start = ((bf16[4,192,768]{2,1,0:T(8,128)(2,1)}), bf16[4,192,768]{2,1,0:T(8,128)(2,1)S(1)}, u32[]{:S(2)}, u32[]{:S(2)}) async-start(bf16[4,192,768]{2,1,0:T(8,128)(2,1)} %fusion.40), calls=%async_computation.1 | async-start | bytes 2359296 | tf_op jit(solution)/shard_map/all_to_all | solution.py:156
  249.1 7.4 %collective-permute-start.8 = (bf16[2,96,512]{2,1,0:T(8,128)(2,1)}, bf16[2,96,512]{2,1,0:T(8,128)(2,1)}, u32[]{:S(2)}, u32[]{:S(2)}) collective-permute-start(bf16[2,96,512]{2,1,0:T(8,128)(2,1)} %collective-permute-done.6), channel_id=1, source_target_pairs={{0,30},{2,0},{4,2},{6,4},{8,6},{10,8},{12,10},{14,12},{16,14},{18,... | collective-permute-start | bytes 589832 | tf_op jit(solution)/shard_map/ppermute | solution.py:179
  253.0 8.2 %collective-permute-start.11 = (bf16[2,96,512]{2,1,0:T(8,128)(2,1)}, bf16[2,96,512]{2,1,0:T(8,128)(2,1)}, u32[]{:S(2)}, u32[]{:S(2)}) collective-permute-start(bf16[2,96,512]{2,1,0:T(8,128)(2,1)} %collective-permute-done.9), channel_id=1, source_target_pairs={{0,2},{2,4},{4,6},{6,8},{8,10},{10,12},{12,14},{14,16},{16,18},{18... | collective-permute-start | bytes 589832 | tf_op jit(solution)/shard_map/ppermute | solution.py:177
  256.5 9.8 %collective-permute-start.10 = (bf16[2,96,512]{2,1,0:T(8,128)(2,1)}, bf16[2,96,512]{2,1,0:T(8,128)(2,1)}, u32[]{:S(2)}, u32[]{:S(2)}) collective-permute-start(bf16[2,96,512]{2,1,0:T(8,128)(2,1)} %collective-permute-done.8), channel_id=1, source_target_pairs={{0,30},{2,0},{4,2},{6,4},{8,6},{10,8},{12,10},{14,12},{16,14},{18,... | collective-permute-start | bytes 589832 | tf_op jit(solution)/shard_map/ppermute | solution.py:179
  261.2 11.4 %collective-permute-start.13 = (bf16[2,96,512]{2,1,0:T(8,128)(2,1)}, bf16[2,96,512]{2,1,0:T(8,128)(2,1)}, u32[]{:S(2)}, u32[]{:S(2)}) collective-permute-start(bf16[2,96,512]{2,1,0:T(8,128)(2,1)} %collective-permute-done.11), channel_id=1, source_target_pairs={{0,2},{2,4},{4,6},{6,8},{8,10},{10,12},{12,14},{14,16},{16,18},{18... | collective-permute-start | bytes 589832 | tf_op jit(solution)/shard_map/ppermute | solution.py:177
  266.2 23.6 %collective-permute-start.12 = (bf16[2,96,512]{2,1,0:T(8,128)(2,1)}, bf16[2,96,512]{2,1,0:T(8,128)(2,1)}, u32[]{:S(2)}, u32[]{:S(2)}) collective-permute-start(bf16[2,96,512]{2,1,0:T(8,128)(2,1)} %collective-permute-done.10), channel_id=1, source_target_pairs={{0,30},{2,0},{4,2},{6,4},{8,6},{10,8},{12,10},{14,12},{16,14},{18,... | collective-permute-start | bytes 589832 | tf_op jit(solution)/shard_map/ppermute | solution.py:179
  272.5 23.0 %collective-permute-start.14 = (bf16[2,96,512]{2,1,0:T(8,128)(2,1)}, bf16[2,96,512]{2,1,0:T(8,128)(2,1)}, u32[]{:S(2)}, u32[]{:S(2)}) collective-permute-start(bf16[2,96,512]{2,1,0:T(8,128)(2,1)} %collective-permute-done.13), channel_id=1, source_target_pairs={{0,2},{2,4},{4,6},{6,8},{8,10},{10,12},{12,14},{14,16},{16,18},{18... | collective-permute-start | bytes 589832 | tf_op jit(solution)/shard_map/ppermute | solution.py:177
  272.5 1.0 copy-start.4
  273.6 1.4 copy-start.11
  280.3 2.6 copy-start.13
  281.6 1.6 copy-start.9
  332.1 3.6 %copy-start.16 = (s32[1,4,4,128]{3,1,2,0:T(4,128)S(1)}, s32[1,4,4,128]{3,1,2,0:T(4,128)}, u32[]{:S(2)}) copy-start(s32[1,4,4,128]{3,1,2,0:T(4,128)} %copy-done.15) | copy-start | bytes 24580
  332.1 3.6 %copy-start.17 = (pred[4,512]{1,0:T(4,128)(4,1)S(1)}, pred[4,512]{1,0:T(4,128)(4,1)}, u32[]{:S(2)}) copy-start(pred[4,512]{1,0:T(4,128)(4,1)} %broadcast_compare_fusion.1) | copy-start | bytes 6148
  336.7 1.1 copy-start.3
  336.8 1.4 copy-start.5
Sparse Core Ops, SparseCore 0:
  11.9 29.8 all-gather.8
  196.1 26.0 reduce-scatter.1
Sparse Core Ops, SparseCore 1:
  198.7 50.4 all-gather.4
  251.3 46.2 all-gather.6
